TPU v7x, 256 devices: a whole 4x4x8 slice. The times are simulated.
256 devices in a mesh: sn: 64 (over y, z, core), rhs: 4 (over x).
Axes of the slice: x: 4, y: 4, z: 8, core: 2. Of those that a mesh axis runs over, the one named last changes fastest.
Arguments:
- leaf_rhs: float32 [256, 1024, 256], P('rhs', 'sn'), may hold values from -6 to 6
- root_rhs: float32 [256, 4096], P('rhs', 'sn'), may hold values from -6 to 6
- leaf_inverse: float32 [1024, 256, 256], P('sn'), as said below
- leaf_offdiagonal_block: float32 [1024, 128, 256], P('sn'), may hold values from -0.125 to 0.125
- update_rows: int32 [1024, 128], P('sn'), may hold values from 0 to 4095, as said below
- leaf_sizes: int32 [1024], P('sn'), may hold values from 1 to 256, 163840 in all
- root_inverse: float32 [4096, 4096], P('sn', 'rhs'), as said below
Outputs:
- leaf_solution: float32 [256, 1024, 256], P('rhs', 'sn')
- root_solution: float32 [256, 4096], P('rhs', 'sn')
Inputs may be any that keep to these rules, and one draw needn't show every extreme that they name: `update_rows`: the 128 rows of one leaf are distinct. `leaf_inverse`: lower triangular with a positive diagonal. `root_inverse`: lower triangular with a positive diagonal.
All inputs are finite; a program needn't handle non-finite values. No bound on the sum of `leaf_sizes` on one device may be relied on, other than what follows from the above.
Results may differ from a plain program's by a relative error of at most 0.00015.
Values sent between devices are 32-bit elements; how exact they have to be, the bound alone decides.
No kernel may reach another device: no remote copies, remote signals or barrier semaphores. Data moves between devices by JAX's collectives and lax.ppermute only.
A program may use at most 64 MiB of HBM per device.

v0:
```python
import jax
import jax.numpy as jnp
from jax import lax
from jax.sharding import PartitionSpec as P


def on_device(
    leaf_rhs, root_rhs, leaf_inverse, leaf_offdiagonal_block, update_rows, leaf_sizes, root_inverse
):
    largest_entry = lax.Precision.HIGHEST
    leaf_count = leaf_inverse.shape[0]
    leaf_width = leaf_inverse.shape[1]
    touched = leaf_offdiagonal_block.shape[1]
    columns = leaf_rhs.shape[0]
    slot_index = lax.broadcasted_iota(jnp.int32, (leaf_count, leaf_width), 1)
    live_mask = (slot_index < leaf_sizes[:, None]).astype(jnp.float32)
    masked = leaf_inverse * live_mask[:, :, None] * live_mask[:, None, :]
    leaf_forward_sweep = jnp.einsum("clt,lst->cls", leaf_rhs, masked, precision=largest_entry)
    update_terms = jnp.einsum(
        "dwu,wqu->dwq", leaf_forward_sweep, leaf_offdiagonal_block, precision=largest_entry
    )
    root_full = lax.all_gather(root_inverse, "rhs", axis=1, tiled=True)
    root_order = root_full.shape[1]
    flat_rows = update_rows.reshape(-1)
    accumulated_sum = (
        jnp.zeros((columns, root_order), jnp.float32)
        .at[:, flat_rows]
        .add(update_terms.reshape(columns, leaf_count * touched))
    )
    shares = lax.psum_scatter(accumulated_sum, "sn", scatter_dimension=1, tiled=True)
    reduced = root_rhs - shares
    forward_root = jnp.einsum(
        "cj,ij->ci",
        lax.all_gather(reduced, "sn", axis=1, tiled=True),
        root_full,
        precision=largest_entry,
    )
    back_terms = jnp.einsum("ci,ij->cj", forward_root, root_full, precision=largest_entry)
    root_solution = lax.psum_scatter(back_terms, "sn", scatter_dimension=1, tiled=True)
    root_values = lax.all_gather(root_solution, "sn", axis=1, tiled=True)
    selected_rows = jnp.take(root_values, flat_rows, axis=1).reshape(columns, leaf_count, touched)
    adjusted_values = leaf_forward_sweep - jnp.einsum(
        "rnv,nvb->rnb", selected_rows, leaf_offdiagonal_block, precision=largest_entry
    )
    leaf_solution = jnp.einsum("cls,lst->clt", adjusted_values, masked, precision=largest_entry)
    return (leaf_solution, root_solution)


def solution(mesh):
    in_specs = (
        P("rhs", "sn", None),
        P("rhs", "sn"),
        P("sn", None, None),
        P("sn", None, None),
        P("sn", None),
        P("sn"),
        P("sn", "rhs"),
    )
    out_specs = (P("rhs", "sn", None), P("rhs", "sn"))
    return jax.shard_map(
        on_device, mesh=mesh, in_specs=in_specs, out_specs=out_specs, check_vma=False
    )
```

profile of v0, /device:TPU:1, one launch (start us, length us, event | category | flops | bytes accessed | tf_op | source)
XLA Modules:
  0.0 512.4 jit_solution(12175633617764443415)
XLA Ops:
  8.0 0.0 copy-start
  8.0 0.0 reduce-scatter.5.cloned.1.call-start
  8.1 0.9 fusion.15
  8.9 7.4 %fusion.6 = f32[64,16,256]{2,0,1:T(8,128)S(1)} fusion(f32[16,256,256]{2,1,0:T(8,128)} %param.9, f32[16,256]{1,0:T(8,128)S(1)} %fusion.15, f32[64,16,256]{2,1,0:T(8,128)} %param.7), kind=kOutput, calls=%fused_computation.11 | convolution fusion | flops 807403520 | bytes 6307840 | tf_op jit(solution)/shard_map/clt,lst->cls/dot_general | solution.py:18
  16.3 0.0 copy-done
  16.3 2.3 convolution_bitcast_fusion.2
  18.6 0.0 copy-start.3
  18.6 0.8 copy.32
  19.4 2.4 copy.21
  21.8 0.0 copy-done.3
  21.8 0.0 copy-start.4
  21.8 13.2 %scatter_custom_fusion = f32[64,4096]{0,1:T(8,128)} fusion(s32[2048]{0:T(1024)S(1)} %bitcast.38, f32[2048,64]{1,0:T(8,128)} %copy.21, f32[]{:T(128)} %constant.18.clone.1), kind=kCustom, calls=%fused_computation.16 | custom fusion | flops 131072 | bytes 1049088 | tf_op jit(solution)/shard_map/scatter-add | solution.py:28
  35.1 0.0 reduce-scatter.5.cloned.1.call-update
  35.1 0.0 all-gather.6.cloned.1.call-start
  35.1 0.5 all-gather.6.cloned.1.call-update
  35.7 0.0 all-gather.4.cloned.1.call-start
  35.7 0.0 copy-done.4
  35.7 0.1 copy.22
  35.8 139.6 %reduce-scatter.5.cloned.1.call-done = f32[64,64]{0,1:T(8,128)} async-done(((f32[64,4096]{0,1:T(8,128)}), f32[64,64]{0,1:T(8,128)}) %reduce-scatter.5.cloned.1.call-update) | async-done | bytes 16400 | tf_op jit(solution)/shard_map/reduce_scatter | solution.py:30
  175.4 1.4 sub.6
  176.7 0.0 all-gather.4.cloned.1.call-update
  176.8 0.2 reduce-scatter.7.cloned.1.call-start
  177.0 0.0 all-gather.6.cloned.1.call-done
  177.0 81.1 %all-gather.4.cloned.1.call-done = f32[64,4096]{0,1:T(8,128)} async-done(((f32[64,64]{0,1:T(8,128)}), f32[64,4096]{0,1:T(8,128)}) %all-gather.4.cloned.1.call-update) | async-done | bytes 1048592 | tf_op jit(solution)/shard_map/all_gather | solution.py:34
  258.2 0.0 copy-start.2
  258.2 5.4 %fusion.17 = f32[64,64]{1,0:T(8,128)S(1)} fusion(f32[64,4096]{0,1:T(8,128)} %all-gather.4.cloned.1.call-done, f32[64,4096]{1,0:T(8,128)} %all-gather.6.cloned.1.call-done), kind=kOutput, calls=%fused_computation.29 | convolution fusion | flops 201326592 | bytes 2113536 | tf_op jit(solution)/shard_map/cj,ij->ci/dot_general | solution.py:32
  263.5 0.0 copy-done.2
  263.5 4.8 convolution_bitcast_fusion
  268.3 0.0 reduce-scatter.7.cloned.1.call-update
  268.3 0.0 all-gather.8.cloned.1.call-start
  268.4 133.5 %reduce-scatter.7.cloned.1.call-done = f32[64,64]{1,0:T(8,128)} async-done(((f32[4096,64]{1,0:T(8,128)}), f32[64,64]{1,0:T(8,128)}) %reduce-scatter.7.cloned.1.call-update) | async-done | bytes 16400
  401.9 0.0 all-gather.8.cloned.1.call-update
  402.0 1.5 copy.27
  403.4 82.8 %all-gather.8.cloned.1.call-done = f32[64,4096]{0,1:T(8,128)} async-done(((f32[64,64]{0,1:T(8,128)}), f32[64,4096]{0,1:T(8,128)}) %all-gather.8.cloned.1.call-update) | async-done | bytes 1048592 | tf_op jit(solution)/shard_map/all_gather | solution.py:40
  486.2 9.2 %gather_fusion = f32[2048,64]{1,0:T(8,128)} fusion(f32[64,4096]{0,1:T(8,128)} %all-gather.8.cloned.1.call-done, s32[2048]{0:T(1024)S(1)} %broadcast_clamp_fusion), kind=kCustom, calls=%fused_computation | custom fusion | bytes 1056768 | tf_op jit(solution)/shard_map/jit(_take)/gather | solution.py:41
  495.4 2.3 copy.24
  497.8 0.0 copy-start.1
  497.8 2.5 fusion.8
  500.3 0.0 copy-done.1
  500.3 3.4 fusion.7
  503.7 1.6 copy.25
  (3 shorter events, 0.0 us)
Async XLA Ops:
  8.0 8.3 %copy-start = (f32[16,128,256]{2,1,0:T(8,128)S(1)}, f32[16,128,256]{2,1,0:T(8,128)}, u32[]{:S(2)}) copy-start(f32[16,128,256]{2,1,0:T(8,128)} %param.10) | copy-start | bytes 6291460
  8.0 167.3 %reduce-scatter.5.cloned.1.call-start = ((), (), s32[]{:S(2)}) async-start(), calls=%async_computation.2 | async-start | bytes 2129920 | tf_op jit(solution)/shard_map/reduce_scatter | solution.py:30
  18.6 3.2 copy-start.3
  21.8 13.9 %copy-start.4 = (f32[64,64]{1,0:T(8,128)S(1)}, f32[64,64]{1,0:T(8,128)}, u32[]{:S(2)}) copy-start(f32[64,64]{1,0:T(8,128)} %param.8) | copy-start | bytes 49156
  35.1 141.9 %all-gather.6.cloned.1.call-start = ((), (), s32[]{:S(2)}) async-start(), calls=%async_computation.4 | async-start | bytes 1310720 | tf_op jit(solution)/shard_map/all_gather | solution.py:22
  35.7 222.5 %all-gather.4.cloned.1.call-start = ((), (), s32[]{:S(2)}) async-start(), calls=%async_computation.3 | async-start | bytes 2129920 | tf_op jit(solution)/shard_map/all_gather | solution.py:34
  176.8 225.2 %reduce-scatter.7.cloned.1.call-start = ((), (), s32[]{:S(2)}) async-start(), calls=%async_computation.6 | async-start | bytes 2129920
  258.2 5.4 %copy-start.2 = (f32[64,4096]{1,0:T(8,128)S(1)}, f32[64,4096]{1,0:T(8,128)}, u32[]{:S(2)}) copy-start(f32[64,4096]{1,0:T(8,128)} %all-gather.6.cloned.1.call-done) | copy-start | bytes 3145732
  268.3 217.9 %all-gather.8.cloned.1.call-start = ((), (), s32[]{:S(2)}) async-start(), calls=%async_computation.5 | async-start | bytes 2129920 | tf_op jit(solution)/shard_map/all_gather | solution.py:40
  497.8 2.5 copy-start.1
Sparse Core Ops, SparseCore 0:
  35.2 140.1 reduce-scatter.4
  268.5 133.4 reduce-scatter.6
  404.7 81.4 all-gather.7
Sparse Core Ops, SparseCore 1:
  37.4 28.2 all-gather.5
  176.8 81.3 all-gather.3
where the time goes:
time: 513 us; the launch traced here: 512 us
  waiting for transfers between devices  438 us (85%)
  matrix products  25.7 us (5%)
  local copies, waits for them, and re-layouts  17.9 us (3%)
  other arithmetic  15.5 us (3%)
  between operations  15.3 us (3%)
    reduce_scatter x1, waiting for transfers between devices, on_device(): lax.psum_scatter(accumulated_sum, 'sn', scatter_dimension=1, tiled=True)  140 us
    unnamed x6, waiting for transfers between devices  134 us
    all_gather x1, waiting for transfers between devices, on_device(): root_values = lax.all_gather(root_solution, 'sn', axis=1, tiled=True)  82.8 us
    all_gather x1, waiting for transfers between devices, on_device(): lax.all_gather(reduced, 'sn', axis=1, tiled=True)  81.1 us
    scatter-add x1, other arithmetic, on_device(): accumulated_sum = jnp.zeros((columns, root_order), jnp.float32).at[:, fla...  13.2 us
    gather x2, local copies, waits for them, and re-layouts, on_device(): jnp.take(root_values, flat_rows, axis=1)  11.5 us
  transfers between devices with their start and end apart: 5, of which 4 were waited for; matrix products, arithmetic and copies ran while one was open for 1% of the time, Pallas kernels for 0%

commit v1 on v0

--- a/solution.py
+++ b/solution.py
@@ -2,6 +2,13 @@
 import jax.numpy as jnp
 from jax import lax
 from jax.sharding import PartitionSpec as P
+
+
+def desk_set(local_array):
+    x_next = lax.axis_size("sn")
+    u_next = jnp.stack(x_next * [local_array])
+    clean = lax.all_to_all(u_next, axis_name="sn", split_axis=0, concat_axis=0)
+    return jnp.concatenate(clean, axis=1)
 
 
 def on_device(
@@ -37,7 +44,7 @@
     )
     back_terms = jnp.einsum("ci,ij->cj", forward_root, root_full, precision=largest_entry)
     root_solution = lax.psum_scatter(back_terms, "sn", scatter_dimension=1, tiled=True)
-    root_values = lax.all_gather(root_solution, "sn", axis=1, tiled=True)
+    root_values = desk_set(root_solution)
     selected_rows = jnp.take(root_values, flat_rows, axis=1).reshape(columns, leaf_count, touched)
     adjusted_values = leaf_forward_sweep - jnp.einsum(
         "rnv,nvb->rnb", selected_rows, leaf_offdiagonal_block, precision=largest_entry

time: 513 us -> 485 us (0.945)
  waiting for transfers between devices: 438 us -> 383 us
  starting transfers between devices: 0.39 us -> 13.5 us
  local copies, waits for them, and re-layouts: 17.9 us -> 26.6 us
  other arithmetic: 15.5 us -> 20.8 us
    all_gather x1 -> x0, waiting for transfers between devices: 82.8 us -> none  [on_device(): root_values = lax.all_gather(root_solution, 'sn', axis=1, tiled=True)]
    all_to_all x0 -> x1, waiting for transfers between devices: none -> 27.7 us  [desk_set(): clean = lax.all_to_all(u_next, axis_name='sn', split_axis=0, concat_axis=0)]
    all_to_all x0 -> x1, starting transfers between devices: none -> 13.1 us  [desk_set(): clean = lax.all_to_all(u_next, axis_name='sn', split_axis=0, concat_axis=0)]
    unnamed x13 -> x18, local copies, waits for them, and re-layouts: 3.14 us -> 11.3 us
    all_to_all x0 -> x1, other arithmetic: none -> 5.32 us  [desk_set(): clean = lax.all_to_all(u_next, axis_name='sn', split_axis=0, concat_axis=0)]
    unnamed x6 -> x5, waiting for transfers between devices: 134 us -> 134 us
  transfers between devices with their start and end apart: 5 -> 5, of which waited for: 4 -> 4; matrix products, arithmetic and copies ran while one was open for 1% -> 0% of each run, Pallas kernels for 0% -> 0%
where the time goes in v1:
time: 485 us
  waiting for transfers between devices  383 us (79%)
  local copies, waits for them, and re-layouts  26.6 us (5%)
  matrix products  25.7 us (5%)
  other arithmetic  20.8 us (4%)
  between operations  15.6 us (3%)
  starting transfers between devices  13.5 us (3%)
    reduce_scatter x1, waiting for transfers between devices, on_device(): lax.psum_scatter(accumulated_sum, 'sn', scatter_dimension=1, tiled=True)  140 us
    unnamed x5, waiting for transfers between devices  134 us
    all_gather x1, waiting for transfers between devices, on_device(): lax.all_gather(reduced, 'sn', axis=1, tiled=True)  81.1 us
    all_to_all x1, waiting for transfers between devices, desk_set(): clean = lax.all_to_all(u_next, axis_name='sn', split_axis=0, concat_axis=0)  27.7 us
    scatter-add x1, other arithmetic, on_device(): accumulated_sum = jnp.zeros((columns, root_order), jnp.float32).at[:, fla...  13.3 us
    all_to_all x1, starting transfers between devices, desk_set(): clean = lax.all_to_all(u_next, axis_name='sn', split_axis=0, concat_axis=0)  13.1 us
    gather x2, local copies, waits for them, and re-layouts, on_device(): jnp.take(root_values, flat_rows, axis=1)  11.6 us
    unnamed x18, local copies, waits for them, and re-layouts  11.3 us
  transfers between devices with their start and end apart: 5, of which 4 were waited for; matrix products, arithmetic and copies ran while one was open for 0% of the time, Pallas kernels for 0%

profile of v1, /device:TPU:1, one launch (start us, length us, event | category | flops | bytes accessed | tf_op | source)
XLA Modules:
  0.0 484.8 jit_solution(8085057431793926604)
XLA Ops:
  8.0 0.0 copy-start
  8.0 0.0 reduce-scatter.5.cloned.1.call-start
  8.1 0.9 fusion.15
  8.9 7.4 %fusion.6 = f32[64,16,256]{2,0,1:T(8,128)S(1)} fusion(f32[16,256,256]{2,1,0:T(8,128)} %param.9, f32[16,256]{1,0:T(8,128)S(1)} %fusion.15, f32[64,16,256]{2,1,0:T(8,128)} %param.7), kind=kOutput, calls=%fused_computation.11 | convolution fusion | flops 807403520 | bytes 6307840 | tf_op jit(solution)/shard_map/clt,lst->cls/dot_general | solution.py:25
  16.3 0.0 copy-done
  16.3 2.3 convolution_bitcast_fusion.2
  18.6 0.0 copy-start.4
  18.6 0.8 copy.32
  19.4 2.4 copy.21
  21.8 0.0 copy-done.4
  21.8 0.0 copy-start.5
  21.8 13.3 %scatter_custom_fusion = f32[64,4096]{0,1:T(8,128)} fusion(s32[2048]{0:T(1024)S(1)} %bitcast.45, f32[2048,64]{1,0:T(8,128)} %copy.21, f32[]{:T(128)} %constant.18.clone.1), kind=kCustom, calls=%fused_computation.16 | custom fusion | flops 131072 | bytes 1049088 | tf_op jit(solution)/shard_map/scatter-add | solution.py:35
  35.1 0.0 reduce-scatter.5.cloned.1.call-update
  35.1 0.0 all-gather.5.cloned.1.call-start
  35.2 0.5 all-gather.5.cloned.1.call-update
  35.7 0.0 all-gather.3.cloned.1.call-start
  35.7 0.0 copy-done.5
  35.7 0.1 copy.22
  35.8 139.6 %reduce-scatter.5.cloned.1.call-done = f32[64,64]{0,1:T(8,128)} async-done(((f32[64,4096]{0,1:T(8,128)}), f32[64,64]{0,1:T(8,128)}) %reduce-scatter.5.cloned.1.call-update) | async-done | bytes 16400 | tf_op jit(solution)/shard_map/reduce_scatter | solution.py:37
  175.4 1.4 sub.6
  176.8 0.0 all-gather.3.cloned.1.call-update
  176.8 0.2 reduce-scatter.7.cloned.1.call-start
  177.0 0.0 all-gather.5.cloned.1.call-done
  177.1 81.1 %all-gather.3.cloned.1.call-done = f32[64,4096]{0,1:T(8,128)} async-done(((f32[64,64]{0,1:T(8,128)}), f32[64,4096]{0,1:T(8,128)}) %all-gather.3.cloned.1.call-update) | async-done | bytes 1048592 | tf_op jit(solution)/shard_map/all_gather | solution.py:41
  258.2 0.0 copy-start.2
  258.2 5.4 %fusion.17 = f32[64,64]{1,0:T(8,128)S(1)} fusion(f32[64,4096]{0,1:T(8,128)} %all-gather.3.cloned.1.call-done, f32[64,4096]{1,0:T(8,128)} %all-gather.5.cloned.1.call-done), kind=kOutput, calls=%fused_computation.30 | convolution fusion | flops 201326592 | bytes 2113536 | tf_op jit(solution)/shard_map/cj,ij->ci/dot_general | solution.py:39
  263.6 0.0 copy-done.2
  263.6 4.8 convolution_bitcast_fusion
  268.4 0.0 reduce-scatter.7.cloned.1.call-update
  268.4 133.6 %reduce-scatter.7.cloned.1.call-done = f32[64,64]{1,0:T(8,128)} async-done(((f32[4096,64]{1,0:T(8,128)}), f32[64,64]{1,0:T(8,128)}) %reduce-scatter.7.cloned.1.call-update) | async-done | bytes 16400
  402.0 2.4 broadcast_bitcast_fusion
  404.3 0.0 copy-start.3
  404.3 3.4 reshape.116
  407.8 13.1 %all-to-all-start = ((f32[64,1,4096]{2,1,0:T(1,128)}), f32[64,1,4096]{2,1,0:T(1,128)}, u32[]{:S(2)}, u32[]{:S(2)}) async-start(f32[64,1,4096]{2,1,0:T(1,128)} %reshape.116), calls=%async_computation.1 | async-start | bytes 2097152 | tf_op jit(solution)/shard_map/all_to_all | solution.py:10
  420.9 0.0 copy-done.3
  420.9 0.7 copy.27
  421.6 27.7 %all-to-all-done = f32[64,1,4096]{2,1,0:T(1,128)} async-done(((f32[64,1,4096]{2,1,0:T(1,128)}), f32[64,1,4096]{2,1,0:T(1,128)}, u32[]{:S(2)}, u32[]{:S(2)}) %all-to-all-start) | async-done | bytes 1048608 | tf_op jit(solution)/shard_map/all_to_all | solution.py:10
  449.3 0.5 broadcast.56
  449.9 5.3 %reduce = f32[64,4096]{1,0:T(8,128)} reduce(f32[64,1,4096]{2,1,0:T(1,128)} %all-to-all-done, f32[]{:T(128)} %broadcast.56), dimensions={1}, to_apply=%all_to_all.3.reduce_sub_computation | reduce | bytes 2097156 | tf_op jit(solution)/shard_map/all_to_all | solution.py:10
  455.2 3.1 reshape.117
  458.3 9.2 %gather_fusion = f32[2048,64]{1,0:T(8,128)} fusion(f32[64,4096]{0,1:T(8,128)} %bitcast.39, s32[2048]{0:T(1024)S(1)} %broadcast_clamp_fusion), kind=kCustom, calls=%fused_computation | custom fusion | bytes 1056768 | tf_op jit(solution)/shard_map/jit(_take)/gather | solution.py:48
  467.5 2.3 copy.24
  469.9 0.0 copy-start.1
  469.9 2.5 fusion.8
  472.4 0.0 copy-done.1
  472.4 3.4 fusion.7
  475.8 1.6 copy.25
  (3 shorter events, 0.0 us)
Async XLA Ops:
  8.0 8.3 %copy-start = (f32[16,128,256]{2,1,0:T(8,128)S(1)}, f32[16,128,256]{2,1,0:T(8,128)}, u32[]{:S(2)}) copy-start(f32[16,128,256]{2,1,0:T(8,128)} %param.10) | copy-start | bytes 6291460
  8.0 167.4 %reduce-scatter.5.cloned.1.call-start = ((), (), s32[]{:S(2)}) async-start(), calls=%async_computation.3 | async-start | bytes 2129920 | tf_op jit(solution)/shard_map/reduce_scatter | solution.py:37
  18.6 3.2 copy-start.4
  21.8 13.9 %copy-start.5 = (f32[64,64]{1,0:T(8,128)S(1)}, f32[64,64]{1,0:T(8,128)}, u32[]{:S(2)}) copy-start(f32[64,64]{1,0:T(8,128)} %param.8) | copy-start | bytes 49156
  35.1 141.9 %all-gather.5.cloned.1.call-start = ((), (), s32[]{:S(2)}) async-start(), calls=%async_computation.5 | async-start | bytes 1310720 | tf_op jit(solution)/shard_map/all_gather | solution.py:29
  35.7 222.5 %all-gather.3.cloned.1.call-start = ((), (), s32[]{:S(2)}) async-start(), calls=%async_computation.4 | async-start | bytes 2129920 | tf_op jit(solution)/shard_map/all_gather | solution.py:41
  176.8 225.2 %reduce-scatter.7.cloned.1.call-start = ((), (), s32[]{:S(2)}) async-start(), calls=%async_computation.6 | async-start | bytes 2129920
  258.2 5.4 %copy-start.2 = (f32[64,4096]{1,0:T(8,128)S(1)}, f32[64,4096]{1,0:T(8,128)}, u32[]{:S(2)}) copy-start(f32[64,4096]{1,0:T(8,128)} %all-gather.5.cloned.1.call-done) | copy-start | bytes 3145732
  404.3 16.6 %copy-start.3 = (f32[64,64]{1,0:T(8,128)S(1)}, f32[64,64]{1,0:T(8,128)}, u32[]{:S(2)}) copy-start(f32[64,64]{1,0:T(8,128)} %reduce-scatter.7.cloned.1.call-done) | copy-start | bytes 49156
  407.8 41.6 %all-to-all-start = ((f32[64,1,4096]{2,1,0:T(1,128)}), f32[64,1,4096]{2,1,0:T(1,128)}, u32[]{:S(2)}, u32[]{:S(2)}) async-start(f32[64,1,4096]{2,1,0:T(1,128)} %reshape.116), calls=%async_computation.1 | async-start | bytes 2097152 | tf_op jit(solution)/shard_map/all_to_all | solution.py:10
  469.9 2.5 copy-start.1
Sparse Core Ops, SparseCore 0:
  35.2 140.1 reduce-scatter.4
  268.5 133.4 reduce-scatter.6
Sparse Core Ops, SparseCore 1:
  37.4 28.2 all-gather.4
  176.9 81.3 all-gather.2
